TPU v7x, 256 devices: a whole 4x4x8 slice. The times are simulated.
256 devices in a mesh: ctx: 16 (over z_lo, x, core), tp: 16 (over z_hi, y).
Axes of the slice: x: 4, y: 4, z: 8 (z_hi: 4, z_lo: 2; z = z_hi * 2 + z_lo), core: 2. Of those that a mesh axis runs over, the one named last changes fastest.
Arguments:
- tokens: bfloat16 [8192, 8192], P('ctx'), may hold values from -40 to 40
- doc_lengths: int32 [8], replicated, may hold values from 1 to 4096, 8192 in all
- w_query: bfloat16 [8192, 4096], P('ctx', 'tp'), may hold values from -0.0625 to 0.0625
- w_key: bfloat16 [8192, 512], P('ctx', 'tp'), may hold values from -0.0625 to 0.0625
- w_value: bfloat16 [8192, 512], P('ctx', 'tp'), may hold values from -0.0625 to 0.0625
- w_output: bfloat16 [4096, 8192], P('tp', 'ctx'), may hold values from -0.09375 to 0.09375
Outputs:
- layer_out: bfloat16 [8192, 8192], P(('ctx', 'tp'))
Inputs may be any that keep to these rules, and one draw needn't show every extreme that they name: `doc_lengths`: the 8 documents lie in order in the sequence, their lengths sum to 8192 and the longest has exactly 4096 tokens.
All inputs are finite; a program needn't handle non-finite values.
Results may differ from a plain program's by a relative error of at most 0.015.
Values may be sent and summed in bfloat16 or wider, within the bound.
No kernel may reach another device: no remote copies, remote signals or barrier semaphores. Data moves between devices by JAX's collectives and lax.ppermute only.
A program may use at most 64 MiB of HBM per device.

v0:
```python
import jax
import jax.numpy as jnp
from jax import lax
from jax.sharding import PartitionSpec as P

HD = 128
HEADS = 32
KVH = 4
DOC_MOST = 4096
rope_base = 500000.0


def rotate(field, positions):
    half_dim = field.shape[-1] // 2
    inverse_freq = rope_base ** (-2.0 * jnp.arange(half_dim, dtype=jnp.float32) / field.shape[-1])
    angles = positions.astype(jnp.float32)[:, None] * inverse_freq[None, :]
    cosine = jnp.cos(angles)[:, None, :]
    sine_part = jnp.sin(angles)[:, None, :]
    first_half = field[..., :half_dim]
    second_half = field[..., half_dim:]
    return jnp.concatenate(
        [
            first_half * cosine - second_half * sine_part,
            second_half * cosine + first_half * sine_part,
        ],
        axis=-1,
    )


def doc_of(positions, doc_starts):
    return jnp.sum((positions[:, None] >= doc_starts[None, :]).astype(jnp.int32), axis=1)


def on_device(tokens, doc_lengths, w_query, w_key, w_value, w_output):
    tok_rows = tokens.shape[0]
    n_tp = lax.axis_size("tp")
    ctx_index = lax.axis_index("ctx")
    tp_index = lax.axis_index("tp")
    first_row = ctx_index * tok_rows
    positions = first_row + jnp.arange(tok_rows, dtype=jnp.int32)
    doc_starts = jnp.cumsum(doc_lengths) - doc_lengths
    doc_ids = doc_of(positions, doc_starts)
    q_cols = w_query.shape[1]
    k_cols = w_key.shape[1]
    w_kv = jnp.concatenate([w_key, w_value], axis=1)
    n_ctx_all = lax.axis_size("ctx")
    ring = [w_kv]
    for shift in range(1, n_ctx_all):
        ring.append(
            lax.ppermute(w_kv, "ctx", [(i, (i + shift) % n_ctx_all) for i in range(n_ctx_all)])
        )
    ring = jnp.stack(ring)
    sources = (ctx_index - jnp.arange(n_ctx_all, dtype=jnp.int32)) % n_ctx_all
    w_kv_full = jnp.take(ring, sources, axis=0).reshape(n_ctx_all * tok_rows, w_kv.shape[1])
    kv_local = jnp.dot(tokens, w_kv_full, preferred_element_type=jnp.float32).astype(jnp.bfloat16)
    w_q_full = lax.all_gather(w_query, "ctx", axis=0, tiled=True)
    query_sum = jnp.dot(tokens, w_q_full, preferred_element_type=jnp.float32)
    heads_dev = q_cols // HD
    query = rotate(query_sum.reshape(tok_rows, heads_dev, HD), positions).astype(jnp.bfloat16)
    dd = k_cols // KVH
    group = HEADS // KVH
    kv_local = kv_local.reshape(tok_rows, 2, dd, KVH)
    dest_heads = jnp.arange(n_tp, dtype=jnp.int32) * heads_dev // group
    pieces = jnp.take(kv_local, dest_heads, axis=3)
    pieces = jnp.transpose(pieces, (3, 0, 1, 2))
    got = lax.all_to_all(pieces, "tp", 0, 0, tiled=False)
    kv_own = jnp.transpose(got, (1, 2, 0, 3)).reshape(tok_rows, 2, n_tp * dd)
    key_raw = kv_own[:, 0, :]
    value_own = kv_own[:, 1, :]
    key_rot = rotate(key_raw.astype(jnp.float32)[:, None, :], positions)[:, 0, :].astype(
        jnp.bfloat16
    )
    kv_rows_local = jnp.concatenate([key_rot, value_own], axis=1)
    n_ctx = lax.axis_size("ctx")
    back = min(n_ctx - 1, -(-(DOC_MOST - 1) // tok_rows))
    slots = []
    for shift in range(back, 0, -1):
        slots.append(
            lax.ppermute(kv_rows_local, "ctx", [(i, i + shift) for i in range(n_ctx - shift)])
        )
    slots.append(kv_rows_local)
    kv_win = jnp.concatenate(slots, axis=0)
    window = kv_win.shape[0]
    key_start = (ctx_index - back) * tok_rows
    key_win = kv_win[:, :HD]
    value_win = kv_win[:, HD:]
    key_positions = key_start + jnp.arange(window, dtype=jnp.int32)
    key_docs = jnp.where(key_positions >= 0, doc_of(key_positions, doc_starts), -1)
    score_scale = HD ** (-0.5)
    n_split = 2
    part_rows = tok_rows // n_split
    q_parts = jnp.transpose(query, (1, 0, 2)).reshape(heads_dev * n_split, part_rows, HD)
    pos_parts = jnp.tile(positions.reshape(n_split, part_rows), (heads_dev, 1))
    doc_parts = jnp.tile(doc_ids.reshape(n_split, part_rows), (heads_dev, 1))

    def one_part(args):
        q_part, pos_part, doc_part = args
        allowed = (key_positions[None, :] <= pos_part[:, None]) & (
            key_docs[None, :] == doc_part[:, None]
        )
        scores = jnp.dot(q_part, key_win.T, preferred_element_type=jnp.float32) * score_scale
        masked = jnp.where(allowed, scores, -jnp.inf)
        row_max = jnp.max(masked, axis=-1, keepdims=True)
        expo = jnp.where(allowed, jnp.exp(masked - row_max), 0.0)
        row_total = jnp.sum(expo, axis=-1, keepdims=True)
        mixed = jnp.dot(expo.astype(jnp.bfloat16), value_win, preferred_element_type=jnp.float32)
        return (mixed / row_total).astype(jnp.bfloat16)

    attended = lax.map(one_part, (q_parts, pos_parts, doc_parts))
    attended = attended.reshape(heads_dev, tok_rows, HD)
    attended = jnp.transpose(attended, (1, 0, 2)).reshape(tok_rows, heads_dev * HD)
    w_moved = lax.ppermute(
        w_output,
        ("ctx", "tp"),
        [(c * n_tp + t, t * n_tp + c) for c in range(n_ctx_all) for t in range(n_tp)],
    )
    w_chunk = lax.all_gather(w_moved, "ctx", axis=0, tiled=True)
    attended_all = lax.all_gather(attended, "tp", axis=1, tiled=True)
    out_chunk = jnp.dot(attended_all, w_chunk, preferred_element_type=jnp.float32).astype(
        jnp.bfloat16
    )
    chunk = out_chunk.shape[1]
    out_rows = tok_rows // n_tp
    sent = out_chunk.reshape(n_tp, out_rows, chunk)
    got_rows = lax.all_to_all(sent, "tp", 0, 0, tiled=False)
    return jnp.transpose(got_rows, (1, 0, 2)).reshape(out_rows, n_tp * chunk)


def solution(mesh):
    placed = (P("ctx", None), P(), P("ctx", "tp"), P("ctx", "tp"), P("ctx", "tp"), P("tp", "ctx"))
    return jax.shard_map(
        on_device, mesh=mesh, in_specs=placed, out_specs=P(("ctx", "tp"), None), check_vma=False
    )
```

profile of v0, /device:TPU:6, one launch (start us, length us, event | category | flops | bytes accessed | tf_op | source)
XLA Modules:
  0.0 282.9 jit_solution(1578596560247495090)
XLA Ops:
  10.6 2.4 collective-permute-start.2
  13.0 2.4 collective-permute-start.3
  21.6 2.7 collective-permute-start.9
  27.5 2.1 collective-permute-start.12
  31.9 10.3 %collective-permute-start.23 = (bf16[256,512]{1,0:T(8,128)(2,1)}, bf16[256,512]{1,0:T(8,128)(2,1)S(1)}, u32[]{:S(2)}, u32[]{:S(2)}) collective-permute-start(bf16[256,512]{1,0:T(8,128)(2,1)} %param.13), channel_id=1, source_target_pairs={{0,0},{1,16},{2,32},{3,48},{4,64},{5,80},{6,96},{7,112},{8,128},{9... | collective-permute-start | bytes 786440 | tf_op jit(solution)/shard_map/ppermute | solution.py:112
  44.8 6.2 %fusion.23 = bf16[512,64]{0,1:T(8,128)(2,1)S(1)} fusion(bf16[512,8192]{1,0:T(8,128)(2,1)} %param.8, bf16[8192,64]{0,1:T(8,128)(2,1)S(1)} %bitcast.100, pred[8192]{0:T(1024)(128)(4,1)S(1)} %bitcast.113), kind=kOutput, calls=%fused_computation.23 | convolution fusion | flops 537427968 | bytes 9510912 | tf_op jit(solution)/shard_map/dot_general | solution.py:55
  52.4 15.2 %all-to-all-start = ((bf16[16,512,2,8]{1,3,2,0:T(8,128)(2,1)}), bf16[16,512,2,8]{1,3,2,0:T(8,128)(2,1)S(1)}, u32[]{:S(2)}, u32[]{:S(2)}) async-start(bf16[16,512,2,8]{1,3,2,0:T(8,128)(2,1)} %broadcast_select_fusion), calls=%async_computation | async-start | bytes 524288 | tf_op jit(solution)/shard_map/all_to_all | solution.py:66
  69.0 11.6 %all-to-all-done = bf16[16,512,2,8]{1,3,2,0:T(8,128)(2,1)S(1)} async-done(((bf16[16,512,2,8]{1,3,2,0:T(8,128)(2,1)}), bf16[16,512,2,8]{1,3,2,0:T(8,128)(2,1)S(1)}, u32[]{:S(2)}, u32[]{:S(2)}) %all-to-all-start) | async-done | bytes 262176 | tf_op jit(solution)/shard_map/all_to_all | solution.py:66
  84.7 1.9 collective-permute-start.17
  87.5 1.9 collective-permute-start.18
  89.4 2.7 collective-permute-start.19
  92.1 2.0 collective-permute-start.20
  94.9 2.0 collective-permute-start.21
  97.0 9.4 %collective-permute-done.17 = bf16[512,256]{0,1:T(8,128)(2,1)S(1)} collective-permute-done((bf16[512,256]{0,1:T(8,128)(2,1)S(1)}, bf16[512,256]{0,1:T(8,128)(2,1)S(1)}, u32[]{:S(2)}, u32[]{:S(2)}) %collective-permute-start.17) | collective-permute-done | bytes 262176 | tf_op jit(solution)/shard_map/ppermute | solution.py:79
  106.4 1.9 collective-permute-start.22
  108.3 5.3 %collective-permute-done.18 = bf16[512,256]{0,1:T(8,128)(2,1)S(1)} collective-permute-done((bf16[512,256]{0,1:T(8,128)(2,1)S(1)}, bf16[512,256]{0,1:T(8,128)(2,1)S(1)}, u32[]{:S(2)}, u32[]{:S(2)}) %collective-permute-start.18) | collective-permute-done | bytes 262176 | tf_op jit(solution)/shard_map/ppermute | solution.py:79
  113.6 11.2 %collective-permute-done.19 = bf16[512,256]{0,1:T(8,128)(2,1)S(1)} collective-permute-done((bf16[512,256]{0,1:T(8,128)(2,1)S(1)}, bf16[512,256]{0,1:T(8,128)(2,1)S(1)}, u32[]{:S(2)}, u32[]{:S(2)}) %collective-permute-start.19) | collective-permute-done | bytes 262176 | tf_op jit(solution)/shard_map/ppermute | solution.py:79
  124.8 11.4 %collective-permute-done.20 = bf16[512,256]{0,1:T(8,128)(2,1)S(1)} collective-permute-done((bf16[512,256]{0,1:T(8,128)(2,1)S(1)}, bf16[512,256]{0,1:T(8,128)(2,1)S(1)}, u32[]{:S(2)}, u32[]{:S(2)}) %collective-permute-start.20) | collective-permute-done | bytes 262176 | tf_op jit(solution)/shard_map/ppermute | solution.py:79
  136.2 6.4 %collective-permute-done.21 = bf16[512,256]{0,1:T(8,128)(2,1)S(1)} collective-permute-done((bf16[512,256]{0,1:T(8,128)(2,1)S(1)}, bf16[512,256]{0,1:T(8,128)(2,1)S(1)}, u32[]{:S(2)}, u32[]{:S(2)}) %collective-permute-start.21) | collective-permute-done | bytes 262176 | tf_op jit(solution)/shard_map/ppermute | solution.py:79
  144.5 7.0 %fusion.43 = f32[512,256]{0,1:T(8,128)S(1)} fusion(bf16[512,8192]{1,0:T(8,128)(2,1)} %param.8, bf16[8192,256]{1,0:T(8,128)(2,1)} %all-gather.4.cloned.1.call-done), kind=kOutput, calls=%fused_computation.114 | convolution fusion | flops 2147483648 | bytes 13107200 | tf_op jit(solution)/shard_map/dot_general | solution.py:57
  151.9 17.3 %while.11 = (s32[]{:T(128)}, bf16[4,256,128]{2,1,0:T(8,128)(2,1)S(1)}, s32[4,256]{1,0:T(4,128)S(1)}, s32[4608]{0:T(1024)S(1)}, s32[4,256]{1,0:T(4,128)S(1)}, /*i...) while((s32[]{:T(128)}, ...), condition=%wide.region_6.7_spmd.clone, body=%wide.region_3.6_spmd.clone.sunk | while | flops 625283072 | bytes 16798836 | solution.py:109
  170.0 74.1 %all-gather.6.cloned.1.call-done = bf16[512,4096]{0,1:T(8,128)(2,1)} async-done(((bf16[512,256]{0,1:T(8,128)(2,1)}), bf16[512,4096]{0,1:T(8,128)(2,1)}) %all-gather.6.cloned.1.call-update) | async-done | bytes 4194320 | tf_op jit(solution)/shard_map/all_gather | solution.py:118
  244.2 5.8 %convolution_convert_fusion = bf16[512,512]{1,0:T(8,128)(2,1)S(1)} fusion(bf16[512,4096]{0,1:T(8,128)(2,1)} %all-gather.6.cloned.1.call-done, bf16[4096,512]{1,0:T(8,128)(2,1)} %all-gather.8.cloned.1.call-done), kind=kOutput, calls=%fused_computation.21 | convolution fusion | flops 2147745792 | bytes 8912896 | tf_op jit(solution)/shard_map/dot_general | solution.py:119
  250.0 25.6 %all_to_all.10 = bf16[16,32,512]{2,1,0:T(8,128)(2,1)S(1)} all-to-all(bf16[16,32,512]{2,1,0:T(8,128)(2,1)S(1)} %bitcast.104), channel_id=1, replica_groups=mesh['ctx'=16,'tp'=16] {'tp'}, dimensions={0} | all-to-all | bytes 1048576 | tf_op jit(solution)/shard_map/all_to_all | solution.py:125
  (140 shorter events, 47.6 us)
Async XLA Ops:
  6.5 137.9 %all-gather.4.cloned.1.call-start = ((), (), s32[]{:S(2)}) async-start(), calls=%async_computation.2 | async-start | bytes 4456448 | tf_op jit(solution)/shard_map/all_gather | solution.py:56
  8.8 8.5 %collective-permute-start = (bf16[512,64]{0,1:T(8,128)(2,1)S(1)}, bf16[512,64]{0,1:T(8,128)(2,1)S(1)}, u32[]{:S(2)}, u32[]{:S(2)}) collective-permute-start(bf16[512,64]{0,1:T(8,128)(2,1)S(1)} %constant_dynamic-update-slice_fusion), channel_id=1, source_target_pairs={{0,16},{16,32},{32,48},{48,64},{64,80},{80,96},{96,112},{112,128},... | collective-permute-start | bytes 196616 | tf_op jit(solution)/shard_map/ppermute | solution.py:50
  8.8 9.8 %collective-permute-start.1 = (bf16[512,64]{0,1:T(8,128)(2,1)S(1)}, bf16[512,64]{0,1:T(8,128)(2,1)S(1)}, u32[]{:S(2)}, u32[]{:S(2)}) collective-permute-start(bf16[512,64]{0,1:T(8,128)(2,1)S(1)} %constant_dynamic-update-slice_fusion), channel_id=1, source_target_pairs={{0,32},{16,48},{32,64},{48,80},{64,96},{80,112},{96,128},{112,144}... | collective-permute-start | bytes 196616 | tf_op jit(solution)/shard_map/ppermute | solution.py:50
  10.6 9.3 %collective-permute-start.2 = (bf16[512,64]{0,1:T(8,128)(2,1)S(1)}, bf16[512,64]{0,1:T(8,128)(2,1)S(1)}, u32[]{:S(2)}, u32[]{:S(2)}) collective-permute-start(bf16[512,64]{0,1:T(8,128)(2,1)S(1)} %constant_dynamic-update-slice_fusion), channel_id=1, source_target_pairs={{0,48},{16,64},{32,80},{48,96},{64,112},{80,128},{96,144},{112,160... | collective-permute-start | bytes 196616 | tf_op jit(solution)/shard_map/ppermute | solution.py:50
  13.0 8.4 %collective-permute-start.3 = (bf16[512,64]{0,1:T(8,128)(2,1)S(1)}, bf16[512,64]{0,1:T(8,128)(2,1)S(1)}, u32[]{:S(2)}, u32[]{:S(2)}) collective-permute-start(bf16[512,64]{0,1:T(8,128)(2,1)S(1)} %constant_dynamic-update-slice_fusion), channel_id=1, source_target_pairs={{0,64},{16,80},{32,96},{48,112},{64,128},{80,144},{96,160},{112,17... | collective-permute-start | bytes 196616 | tf_op jit(solution)/shard_map/ppermute | solution.py:50
  21.5 8.2 %collective-permute-start.8 = (bf16[512,64]{0,1:T(8,128)(2,1)S(1)}, bf16[512,64]{0,1:T(8,128)(2,1)S(1)}, u32[]{:S(2)}, u32[]{:S(2)}) collective-permute-start(bf16[512,64]{0,1:T(8,128)(2,1)S(1)} %constant_dynamic-update-slice_fusion), channel_id=1, source_target_pairs={{0,144},{16,160},{32,176},{48,192},{64,208},{80,224},{96,240},{112... | collective-permute-start | bytes 196616 | tf_op jit(solution)/shard_map/ppermute | solution.py:50
  21.6 8.4 %collective-permute-start.9 = (bf16[512,64]{0,1:T(8,128)(2,1)S(1)}, bf16[512,64]{0,1:T(8,128)(2,1)S(1)}, u32[]{:S(2)}, u32[]{:S(2)}) collective-permute-start(bf16[512,64]{0,1:T(8,128)(2,1)S(1)} %constant_dynamic-update-slice_fusion), channel_id=1, source_target_pairs={{0,160},{16,176},{32,192},{48,208},{64,224},{80,240},{96,0},{112,1... | collective-permute-start | bytes 196616 | tf_op jit(solution)/shard_map/ppermute | solution.py:50
  24.3 7.6 %collective-permute-start.10 = (bf16[512,64]{0,1:T(8,128)(2,1)S(1)}, bf16[512,64]{0,1:T(8,128)(2,1)S(1)}, u32[]{:S(2)}, u32[]{:S(2)}) collective-permute-start(bf16[512,64]{0,1:T(8,128)(2,1)S(1)} %constant_dynamic-update-slice_fusion), channel_id=1, source_target_pairs={{0,176},{16,192},{32,208},{48,224},{64,240},{80,0},{96,16},{112,32... | collective-permute-start | bytes 196616 | tf_op jit(solution)/shard_map/ppermute | solution.py:50
  25.8 16.4 %collective-permute-start.11 = (bf16[512,64]{0,1:T(8,128)(2,1)S(1)}, bf16[512,64]{0,1:T(8,128)(2,1)S(1)}, u32[]{:S(2)}, u32[]{:S(2)}) collective-permute-start(bf16[512,64]{0,1:T(8,128)(2,1)S(1)} %constant_dynamic-update-slice_fusion), channel_id=1, source_target_pairs={{0,192},{16,208},{32,224},{48,240},{64,0},{80,16},{96,32},{112,48}... | collective-permute-start | bytes 196616 | tf_op jit(solution)/shard_map/ppermute | solution.py:50
  27.5 14.8 %collective-permute-start.12 = (bf16[512,64]{0,1:T(8,128)(2,1)S(1)}, bf16[512,64]{0,1:T(8,128)(2,1)S(1)}, u32[]{:S(2)}, u32[]{:S(2)}) collective-permute-start(bf16[512,64]{0,1:T(8,128)(2,1)S(1)} %constant_dynamic-update-slice_fusion), channel_id=1, source_target_pairs={{0,208},{16,224},{32,240},{48,0},{64,16},{80,32},{96,48},{112,64},... | collective-permute-start | bytes 196616 | tf_op jit(solution)/shard_map/ppermute | solution.py:50
  29.6 14.4 %collective-permute-start.13 = (bf16[512,64]{0,1:T(8,128)(2,1)S(1)}, bf16[512,64]{0,1:T(8,128)(2,1)S(1)}, u32[]{:S(2)}, u32[]{:S(2)}) collective-permute-start(bf16[512,64]{0,1:T(8,128)(2,1)S(1)} %constant_dynamic-update-slice_fusion), channel_id=1, source_target_pairs={{0,224},{16,240},{32,0},{48,16},{64,32},{80,48},{96,64},{112,80},{... | collective-permute-start | bytes 196616 | tf_op jit(solution)/shard_map/ppermute | solution.py:50
  30.0 14.1 %collective-permute-start.14 = (bf16[512,64]{0,1:T(8,128)(2,1)S(1)}, bf16[512,64]{0,1:T(8,128)(2,1)S(1)}, u32[]{:S(2)}, u32[]{:S(2)}) collective-permute-start(bf16[512,64]{0,1:T(8,128)(2,1)S(1)} %constant_dynamic-update-slice_fusion), channel_id=1, source_target_pairs={{0,240},{16,0},{32,16},{48,32},{64,48},{80,64},{96,80},{112,96},{1... | collective-permute-start | bytes 196616 | tf_op jit(solution)/shard_map/ppermute | solution.py:50
  31.9 54.7 %collective-permute-start.23 = (bf16[256,512]{1,0:T(8,128)(2,1)}, bf16[256,512]{1,0:T(8,128)(2,1)S(1)}, u32[]{:S(2)}, u32[]{:S(2)}) collective-permute-start(bf16[256,512]{1,0:T(8,128)(2,1)} %param.13), channel_id=1, source_target_pairs={{0,0},{1,16},{2,32},{3,48},{4,64},{5,80},{6,96},{7,112},{8,128},{9... | collective-permute-start | bytes 786440 | tf_op jit(solution)/shard_map/ppermute | solution.py:112
  52.4 28.3 %all-to-all-start = ((bf16[16,512,2,8]{1,3,2,0:T(8,128)(2,1)}), bf16[16,512,2,8]{1,3,2,0:T(8,128)(2,1)S(1)}, u32[]{:S(2)}, u32[]{:S(2)}) async-start(bf16[16,512,2,8]{1,3,2,0:T(8,128)(2,1)} %broadcast_select_fusion), calls=%async_computation | async-start | bytes 524288 | tf_op jit(solution)/shard_map/all_to_all | solution.py:66
  67.6 102.5 %all-gather.8.cloned.1.call-start = ((), (), s32[]{:S(2)}) async-start(), calls=%async_computation.4 | async-start | bytes 4456448 | tf_op jit(solution)/shard_map/all_gather | solution.py:117
  81.3 10.8 %collective-permute-start.15 = (bf16[512,256]{0,1:T(8,128)(2,1)S(1)}, bf16[512,256]{0,1:T(8,128)(2,1)S(1)}, u32[]{:S(2)}, u32[]{:S(2)}) collective-permute-start(bf16[512,256]{0,1:T(8,128)(2,1)S(1)} %pad_maximum_fusion), channel_id=1, source_target_pairs={{0,128},{16,144},{32,160},{48,176},{64,192},{80,208},{96,224},{112... | collective-permute-start | bytes 786440 | tf_op jit(solution)/shard_map/ppermute | solution.py:79
  83.3 11.7 %collective-permute-start.16 = (bf16[512,256]{0,1:T(8,128)(2,1)S(1)}, bf16[512,256]{0,1:T(8,128)(2,1)S(1)}, u32[]{:S(2)}, u32[]{:S(2)}) collective-permute-start(bf16[512,256]{0,1:T(8,128)(2,1)S(1)} %pad_maximum_fusion), channel_id=1, source_target_pairs={{0,112},{16,128},{32,144},{48,160},{64,176},{80,192},{96,208},{112... | collective-permute-start | bytes 786440 | tf_op jit(solution)/shard_map/ppermute | solution.py:79
  84.7 21.7 %collective-permute-start.17 = (bf16[512,256]{0,1:T(8,128)(2,1)S(1)}, bf16[512,256]{0,1:T(8,128)(2,1)S(1)}, u32[]{:S(2)}, u32[]{:S(2)}) collective-permute-start(bf16[512,256]{0,1:T(8,128)(2,1)S(1)} %pad_maximum_fusion), channel_id=1, source_target_pairs={{0,96},{16,112},{32,128},{48,144},{64,160},{80,176},{96,192},{112,... | collective-permute-start | bytes 786440 | tf_op jit(solution)/shard_map/ppermute | solution.py:79
  87.4 156.7 %all-gather.6.cloned.1.call-start = ((), (), s32[]{:S(2)}) async-start(), calls=%async_computation.3 | async-start | bytes 4456448 | tf_op jit(solution)/shard_map/all_gather | solution.py:118
  87.5 26.1 %collective-permute-start.18 = (bf16[512,256]{0,1:T(8,128)(2,1)S(1)}, bf16[512,256]{0,1:T(8,128)(2,1)S(1)}, u32[]{:S(2)}, u32[]{:S(2)}) collective-permute-start(bf16[512,256]{0,1:T(8,128)(2,1)S(1)} %pad_maximum_fusion), channel_id=1, source_target_pairs={{0,80},{16,96},{32,112},{48,128},{64,144},{80,160},{96,176},{112,1... | collective-permute-start | bytes 786440 | tf_op jit(solution)/shard_map/ppermute | solution.py:79
  89.4 35.4 %collective-permute-start.19 = (bf16[512,256]{0,1:T(8,128)(2,1)S(1)}, bf16[512,256]{0,1:T(8,128)(2,1)S(1)}, u32[]{:S(2)}, u32[]{:S(2)}) collective-permute-start(bf16[512,256]{0,1:T(8,128)(2,1)S(1)} %pad_maximum_fusion), channel_id=1, source_target_pairs={{0,64},{16,80},{32,96},{48,112},{64,128},{80,144},{96,160},{112,17... | collective-permute-start | bytes 786440 | tf_op jit(solution)/shard_map/ppermute | solution.py:79
  92.1 44.1 %collective-permute-start.20 = (bf16[512,256]{0,1:T(8,128)(2,1)S(1)}, bf16[512,256]{0,1:T(8,128)(2,1)S(1)}, u32[]{:S(2)}, u32[]{:S(2)}) collective-permute-start(bf16[512,256]{0,1:T(8,128)(2,1)S(1)} %pad_maximum_fusion), channel_id=1, source_target_pairs={{0,48},{16,64},{32,80},{48,96},{64,112},{80,128},{96,144},{112,160... | collective-permute-start | bytes 786440 | tf_op jit(solution)/shard_map/ppermute | solution.py:79
  94.9 47.8 %collective-permute-start.21 = (bf16[512,256]{0,1:T(8,128)(2,1)S(1)}, bf16[512,256]{0,1:T(8,128)(2,1)S(1)}, u32[]{:S(2)}, u32[]{:S(2)}) collective-permute-start(bf16[512,256]{0,1:T(8,128)(2,1)S(1)} %pad_maximum_fusion), channel_id=1, source_target_pairs={{0,32},{16,48},{32,64},{48,80},{64,96},{80,112},{96,128},{112,144}... | collective-permute-start | bytes 786440 | tf_op jit(solution)/shard_map/ppermute | solution.py:79
  106.4 36.3 %collective-permute-start.22 = (bf16[512,256]{0,1:T(8,128)(2,1)S(1)}, bf16[512,256]{0,1:T(8,128)(2,1)S(1)}, u32[]{:S(2)}, u32[]{:S(2)}) collective-permute-start(bf16[512,256]{0,1:T(8,128)(2,1)S(1)} %pad_maximum_fusion), channel_id=1, source_target_pairs={{0,16},{16,32},{32,48},{48,64},{64,80},{80,96},{96,112},{112,128},... | collective-permute-start | bytes 786440 | tf_op jit(solution)/shard_map/ppermute | solution.py:79
  (9 other events, 57.8 us)
Sparse Core Ops, SparseCore 0:
  9.2 57.2 all-gather.3
  87.5 52.1 all-gather.7
  170.1 73.9 all-gather.5
where the time goes:
time: 284 us; the launch traced here: 283 us
  waiting for transfers between devices  134 us (47%)
  starting transfers between devices  60.7 us (21%)
  matrix products  30.3 us (11%)
  blocking collectives  25.6 us (9%)
  between operations  13.7 us (5%)
  other arithmetic  11.1 us (4%)
  local copies, waits for them, and re-layouts  7.47 us (3%)
    all_gather x1, waiting for transfers between devices, on_device(): attended_all = lax.all_gather(attended, 'tp', axis=1, tiled=True)  74.1 us
    ppermute x8, waiting for transfers between devices, on_device(): lax.ppermute(kv_rows_local, 'ctx', [(i, i + shift) for i in range(n_ctx -...  44.5 us
    all_to_all x1, blocking collectives, on_device(): got_rows = lax.all_to_all(sent, 'tp', 0, 0, tiled=False)  25.6 us
    ppermute x15, starting transfers between devices, on_device(): lax.ppermute(w_kv, 'ctx', [(i, (i + shift) % n_ctx_all) for i in range(n_...  20.1 us
    all_to_all x1, starting transfers between devices, on_device(): got = lax.all_to_all(pieces, 'tp', 0, 0, tiled=False)  15.2 us
    ppermute x8, starting transfers between devices, on_device(): lax.ppermute(kv_rows_local, 'ctx', [(i, i + shift) for i in range(n_ctx -...  15 us
    all_to_all x1, waiting for transfers between devices, on_device(): got = lax.all_to_all(pieces, 'tp', 0, 0, tiled=False)  11.6 us
    ppermute x1, starting transfers between devices, on_device(): lax.ppermute(w_output, ('ctx', 'tp'), [(c * n_tp + t, t * n_tp + c) for c...  10.3 us
  transfers between devices with their start and end apart: 28, of which 10 were waited for; matrix products, arithmetic and copies ran while one was open for 15% of the time, Pallas kernels for 0%

commit v1 on v0

--- a/solution.py
+++ b/solution.py
@@ -115,7 +115,9 @@
         [(c * n_tp + t, t * n_tp + c) for c in range(n_ctx_all) for t in range(n_tp)],
     )
     w_chunk = lax.all_gather(w_moved, "ctx", axis=0, tiled=True)
-    attended_all = lax.all_gather(attended, "tp", axis=1, tiled=True)
+    attended_all = jnp.concatenate(
+        lax.all_to_all(jnp.stack([attended] * lax.axis_size("tp")), "tp", 0, 0), axis=1
+    )
     out_chunk = jnp.dot(attended_all, w_chunk, preferred_element_type=jnp.float32).astype(
         jnp.bfloat16
     )

time: 284 us -> 307 us (1.081)
  the two profiles are of different devices: /device:TPU:6 before, /device:TPU:32 now
where the time goes in v1:
time: 307 us; the launch traced here: 306 us
  waiting for transfers between devices  151 us (49%)
  starting transfers between devices  65.7 us (21%)
  matrix products  30.3 us (10%)
  blocking collectives  24.4 us (8%)
  between operations  14 us (5%)
  other arithmetic  11 us (4%)
  local copies, waits for them, and re-layouts  9.17 us (3%)
    all_to_all x1, waiting for transfers between devices, on_device(): lax.all_to_all(jnp.stack([attended] * lax.axis_size('tp')), 'tp', 0, 0)  86.8 us
    ppermute x8, waiting for transfers between devices, on_device(): lax.ppermute(kv_rows_local, 'ctx', [(i, i + shift) for i in range(n_ctx -...  50.5 us
    all_to_all x1, blocking collectives, on_device(): got_rows = lax.all_to_all(sent, 'tp', 0, 0, tiled=False)  24.4 us
    ppermute x15, starting transfers between devices, on_device(): lax.ppermute(w_kv, 'ctx', [(i, (i + shift) % n_ctx_all) for i in range(n_...  22 us
    ppermute x8, starting transfers between devices, on_device(): lax.ppermute(kv_rows_local, 'ctx', [(i, i + shift) for i in range(n_ctx -...  16.3 us
    all_to_all x1, starting transfers between devices, on_device(): got = lax.all_to_all(pieces, 'tp', 0, 0, tiled=False)  14.4 us
    all_to_all x1, waiting for transfers between devices, on_device(): got = lax.all_to_all(pieces, 'tp', 0, 0, tiled=False)  10.3 us
    ppermute x1, starting transfers between devices, on_device(): lax.ppermute(w_output, ('ctx', 'tp'), [(c * n_tp + t, t * n_tp + c) for c...  8.47 us
  transfers between devices with their start and end apart: 28, of which 9 were waited for; matrix products, arithmetic and copies ran while one was open for 14% of the time, Pallas kernels for 0%

profile of v1, /device:TPU:32, one launch (start us, length us, event | category | flops | bytes accessed | tf_op | source)
XLA Modules:
  0.0 305.9 jit_solution(8241838994931125718)
XLA Ops:
  10.3 2.1 collective-permute-start.2
  12.4 2.1 collective-permute-start.3
  17.2 2.9 collective-permute-start.5
  25.8 2.5 collective-permute-start.11
  29.6 2.4 collective-permute-start.13
  33.3 8.5 %collective-permute-start.23 = (bf16[256,512]{1,0:T(8,128)(2,1)}, bf16[256,512]{1,0:T(8,128)(2,1)S(1)}, u32[]{:S(2)}, u32[]{:S(2)}) collective-permute-start(bf16[256,512]{1,0:T(8,128)(2,1)} %param.13), channel_id=1, source_target_pairs={{0,0},{1,16},{2,32},{3,48},{4,64},{5,80},{6,96},{7,112},{8,128},{9... | collective-permute-start | bytes 786440 | tf_op jit(solution)/shard_map/ppermute | solution.py:112
  41.9 2.0 collective-permute-done.14
  44.6 6.2 %fusion.23 = bf16[512,64]{0,1:T(8,128)(2,1)S(1)} fusion(bf16[512,8192]{1,0:T(8,128)(2,1)} %param.8, bf16[8192,64]{0,1:T(8,128)(2,1)S(1)} %bitcast.103, pred[8192]{0:T(1024)(128)(4,1)S(1)} %bitcast.116), kind=kOutput, calls=%fused_computation.23 | convolution fusion | flops 537427968 | bytes 9510912 | tf_op jit(solution)/shard_map/dot_general | solution.py:55
  52.2 14.4 %all-to-all-start = ((bf16[16,512,2,8]{1,3,2,0:T(8,128)(2,1)}), bf16[16,512,2,8]{1,3,2,0:T(8,128)(2,1)S(1)}, u32[]{:S(2)}, u32[]{:S(2)}) async-start(bf16[16,512,2,8]{1,3,2,0:T(8,128)(2,1)} %broadcast_select_fusion), calls=%async_computation | async-start | bytes 524288 | tf_op jit(solution)/shard_map/all_to_all | solution.py:66
  68.0 10.3 %all-to-all-done = bf16[16,512,2,8]{1,3,2,0:T(8,128)(2,1)S(1)} async-done(((bf16[16,512,2,8]{1,3,2,0:T(8,128)(2,1)}), bf16[16,512,2,8]{1,3,2,0:T(8,128)(2,1)S(1)}, u32[]{:S(2)}, u32[]{:S(2)}) %all-to-all-start) | async-done | bytes 262176 | tf_op jit(solution)/shard_map/all_to_all | solution.py:66
  81.0 3.5 %collective-permute-start.16 = (bf16[512,256]{0,1:T(8,128)(2,1)S(1)}, bf16[512,256]{0,1:T(8,128)(2,1)S(1)}, u32[]{:S(2)}, u32[]{:S(2)}) collective-permute-start(bf16[512,256]{0,1:T(8,128)(2,1)S(1)} %pad_maximum_fusion), channel_id=1, source_target_pairs={{0,112},{16,128},{32,144},{48,160},{64,176},{80,192},{96,208},{112... | collective-permute-start | bytes 786440 | tf_op jit(solution)/shard_map/ppermute | solution.py:79
  91.2 1.9 collective-permute-start.20
  95.1 2.2 collective-permute-done.17
  99.3 7.5 %collective-permute-done.19 = bf16[512,256]{0,1:T(8,128)(2,1)S(1)} collective-permute-done((bf16[512,256]{0,1:T(8,128)(2,1)S(1)}, bf16[512,256]{0,1:T(8,128)(2,1)S(1)}, u32[]{:S(2)}, u32[]{:S(2)}) %collective-permute-start.19) | collective-permute-done | bytes 262176 | tf_op jit(solution)/shard_map/ppermute | solution.py:79
  106.8 11.2 %collective-permute-done.20 = bf16[512,256]{0,1:T(8,128)(2,1)S(1)} collective-permute-done((bf16[512,256]{0,1:T(8,128)(2,1)S(1)}, bf16[512,256]{0,1:T(8,128)(2,1)S(1)}, u32[]{:S(2)}, u32[]{:S(2)}) %collective-permute-start.20) | collective-permute-done | bytes 262176 | tf_op jit(solution)/shard_map/ppermute | solution.py:79
  118.1 27.4 %collective-permute-done.21 = bf16[512,256]{0,1:T(8,128)(2,1)S(1)} collective-permute-done((bf16[512,256]{0,1:T(8,128)(2,1)S(1)}, bf16[512,256]{0,1:T(8,128)(2,1)S(1)}, u32[]{:S(2)}, u32[]{:S(2)}) %collective-permute-start.21) | collective-permute-done | bytes 262176 | tf_op jit(solution)/shard_map/ppermute | solution.py:79
  145.5 2.2 collective-permute-done.22
  149.4 7.0 %fusion.43 = f32[512,256]{0,1:T(8,128)S(1)} fusion(bf16[512,8192]{1,0:T(8,128)(2,1)} %param.8, bf16[8192,256]{1,0:T(8,128)(2,1)} %all-gather.3.cloned.1.call-done), kind=kOutput, calls=%fused_computation.114 | convolution fusion | flops 2147483648 | bytes 13107200 | tf_op jit(solution)/shard_map/dot_general | solution.py:57
  156.8 17.3 %while.11 = (s32[]{:T(128)}, bf16[4,256,128]{2,1,0:T(8,128)(2,1)S(1)}, s32[4,256]{1,0:T(4,128)S(1)}, s32[4608]{0:T(1024)S(1)}, s32[4,256]{1,0:T(4,128)S(1)}, /*i...) while((s32[]{:T(128)}, ...), condition=%wide.region_6.7_spmd.clone, body=%wide.region_3.6_spmd.clone.sunk | while | flops 625283072 | bytes 16798836 | solution.py:109
  174.3 2.4 stack.71
  176.7 4.5 %all-to-all-start.1 = ((bf16[16,512,256]{1,2,0:T(8,128)(2,1)}), bf16[16,512,256]{1,2,0:T(8,128)(2,1)}, u32[]{:S(2)}, u32[]{:S(2)}) async-start(bf16[16,512,256]{1,2,0:T(8,128)(2,1)} %stack.71), calls=%async_computation.1 | async-start | bytes 8388608 | tf_op jit(solution)/shard_map/all_to_all | solution.py:119
  181.2 86.8 %all-to-all-done.1 = bf16[16,512,256]{1,2,0:T(8,128)(2,1)} async-done(((bf16[16,512,256]{1,2,0:T(8,128)(2,1)}), bf16[16,512,256]{1,2,0:T(8,128)(2,1)}, u32[]{:S(2)}, u32[]{:S(2)}) %all-to-all-start.1) | async-done | bytes 4194336 | tf_op jit(solution)/shard_map/all_to_all | solution.py:119
  268.0 5.8 %convolution_convert_fusion = bf16[512,512]{1,0:T(8,128)(2,1)S(1)} fusion(bf16[512,4096]{0,1:T(8,128)(2,1)} %bitcast.32, bf16[4096,512]{1,0:T(8,128)(2,1)} %all-gather.5.cloned.1.call-done), kind=kOutput, calls=%fused_computation.21 | convolution fusion | flops 2147745792 | bytes 8912896 | tf_op jit(solution)/shard_map/dot_general | solution.py:121
  273.8 24.4 %all_to_all.15 = bf16[16,32,512]{2,1,0:T(8,128)(2,1)S(1)} all-to-all(bf16[16,32,512]{2,1,0:T(8,128)(2,1)S(1)} %bitcast.107), channel_id=1, replica_groups=mesh['ctx'=16,'tp'=16] {'tp'}, dimensions={0} | all-to-all | bytes 1048576 | tf_op jit(solution)/shard_map/all_to_all | solution.py:127
  (140 shorter events, 51.5 us)
Async XLA Ops:
  6.5 142.9 %all-gather.3.cloned.1.call-start = ((), (), s32[]{:S(2)}) async-start(), calls=%async_computation.3 | async-start | bytes 4456448 | tf_op jit(solution)/shard_map/all_gather | solution.py:56
  8.8 8.4 %collective-permute-start = (bf16[512,64]{0,1:T(8,128)(2,1)S(1)}, bf16[512,64]{0,1:T(8,128)(2,1)S(1)}, u32[]{:S(2)}, u32[]{:S(2)}) collective-permute-start(bf16[512,64]{0,1:T(8,128)(2,1)S(1)} %constant_dynamic-update-slice_fusion), channel_id=1, source_target_pairs={{0,16},{16,32},{32,48},{48,64},{64,80},{80,96},{96,112},{112,128},... | collective-permute-start | bytes 196616 | tf_op jit(solution)/shard_map/ppermute | solution.py:50
  8.8 11.3 %collective-permute-start.1 = (bf16[512,64]{0,1:T(8,128)(2,1)S(1)}, bf16[512,64]{0,1:T(8,128)(2,1)S(1)}, u32[]{:S(2)}, u32[]{:S(2)}) collective-permute-start(bf16[512,64]{0,1:T(8,128)(2,1)S(1)} %constant_dynamic-update-slice_fusion), channel_id=1, source_target_pairs={{0,32},{16,48},{32,64},{48,80},{64,96},{80,112},{96,128},{112,144}... | collective-permute-start | bytes 196616 | tf_op jit(solution)/shard_map/ppermute | solution.py:50
  10.3 9.9 %collective-permute-start.2 = (bf16[512,64]{0,1:T(8,128)(2,1)S(1)}, bf16[512,64]{0,1:T(8,128)(2,1)S(1)}, u32[]{:S(2)}, u32[]{:S(2)}) collective-permute-start(bf16[512,64]{0,1:T(8,128)(2,1)S(1)} %constant_dynamic-update-slice_fusion), channel_id=1, source_target_pairs={{0,48},{16,64},{32,80},{48,96},{64,112},{80,128},{96,144},{112,160... | collective-permute-start | bytes 196616 | tf_op jit(solution)/shard_map/ppermute | solution.py:50
  12.4 9.3 %collective-permute-start.3 = (bf16[512,64]{0,1:T(8,128)(2,1)S(1)}, bf16[512,64]{0,1:T(8,128)(2,1)S(1)}, u32[]{:S(2)}, u32[]{:S(2)}) collective-permute-start(bf16[512,64]{0,1:T(8,128)(2,1)S(1)} %constant_dynamic-update-slice_fusion), channel_id=1, source_target_pairs={{0,64},{16,80},{32,96},{48,112},{64,128},{80,144},{96,160},{112,17... | collective-permute-start | bytes 196616 | tf_op jit(solution)/shard_map/ppermute | solution.py:50
  20.2 8.1 %collective-permute-start.7 = (bf16[512,64]{0,1:T(8,128)(2,1)S(1)}, bf16[512,64]{0,1:T(8,128)(2,1)S(1)}, u32[]{:S(2)}, u32[]{:S(2)}) collective-permute-start(bf16[512,64]{0,1:T(8,128)(2,1)S(1)} %constant_dynamic-update-slice_fusion), channel_id=1, source_target_pairs={{0,128},{16,144},{32,160},{48,176},{64,192},{80,208},{96,224},{112... | collective-permute-start | bytes 196616 | tf_op jit(solution)/shard_map/ppermute | solution.py:50
  22.2 9.9 %collective-permute-start.9 = (bf16[512,64]{0,1:T(8,128)(2,1)S(1)}, bf16[512,64]{0,1:T(8,128)(2,1)S(1)}, u32[]{:S(2)}, u32[]{:S(2)}) collective-permute-start(bf16[512,64]{0,1:T(8,128)(2,1)S(1)} %constant_dynamic-update-slice_fusion), channel_id=1, source_target_pairs={{0,160},{16,176},{32,192},{48,208},{64,224},{80,240},{96,0},{112,1... | collective-permute-start | bytes 196616 | tf_op jit(solution)/shard_map/ppermute | solution.py:50
  24.0 9.3 %collective-permute-start.10 = (bf16[512,64]{0,1:T(8,128)(2,1)S(1)}, bf16[512,64]{0,1:T(8,128)(2,1)S(1)}, u32[]{:S(2)}, u32[]{:S(2)}) collective-permute-start(bf16[512,64]{0,1:T(8,128)(2,1)S(1)} %constant_dynamic-update-slice_fusion), channel_id=1, source_target_pairs={{0,176},{16,192},{32,208},{48,224},{64,240},{80,0},{96,16},{112,32... | collective-permute-start | bytes 196616 | tf_op jit(solution)/shard_map/ppermute | solution.py:50
  25.8 16.0 %collective-permute-start.11 = (bf16[512,64]{0,1:T(8,128)(2,1)S(1)}, bf16[512,64]{0,1:T(8,128)(2,1)S(1)}, u32[]{:S(2)}, u32[]{:S(2)}) collective-permute-start(bf16[512,64]{0,1:T(8,128)(2,1)S(1)} %constant_dynamic-update-slice_fusion), channel_id=1, source_target_pairs={{0,192},{16,208},{32,224},{48,240},{64,0},{80,16},{96,32},{112,48}... | collective-permute-start | bytes 196616 | tf_op jit(solution)/shard_map/ppermute | solution.py:50
  28.3 13.5 %collective-permute-start.12 = (bf16[512,64]{0,1:T(8,128)(2,1)S(1)}, bf16[512,64]{0,1:T(8,128)(2,1)S(1)}, u32[]{:S(2)}, u32[]{:S(2)}) collective-permute-start(bf16[512,64]{0,1:T(8,128)(2,1)S(1)} %constant_dynamic-update-slice_fusion), channel_id=1, source_target_pairs={{0,208},{16,224},{32,240},{48,0},{64,16},{80,32},{96,48},{112,64},... | collective-permute-start | bytes 196616 | tf_op jit(solution)/shard_map/ppermute | solution.py:50
  29.6 12.2 %collective-permute-start.13 = (bf16[512,64]{0,1:T(8,128)(2,1)S(1)}, bf16[512,64]{0,1:T(8,128)(2,1)S(1)}, u32[]{:S(2)}, u32[]{:S(2)}) collective-permute-start(bf16[512,64]{0,1:T(8,128)(2,1)S(1)} %constant_dynamic-update-slice_fusion), channel_id=1, source_target_pairs={{0,224},{16,240},{32,0},{48,16},{64,32},{80,48},{96,64},{112,80},{... | collective-permute-start | bytes 196616 | tf_op jit(solution)/shard_map/ppermute | solution.py:50
  32.0 11.9 %collective-permute-start.14 = (bf16[512,64]{0,1:T(8,128)(2,1)S(1)}, bf16[512,64]{0,1:T(8,128)(2,1)S(1)}, u32[]{:S(2)}, u32[]{:S(2)}) collective-permute-start(bf16[512,64]{0,1:T(8,128)(2,1)S(1)} %constant_dynamic-update-slice_fusion), channel_id=1, source_target_pairs={{0,240},{16,0},{32,16},{48,32},{64,48},{80,64},{96,80},{112,96},{1... | collective-permute-start | bytes 196616 | tf_op jit(solution)/shard_map/ppermute | solution.py:50
  33.3 53.3 %collective-permute-start.23 = (bf16[256,512]{1,0:T(8,128)(2,1)}, bf16[256,512]{1,0:T(8,128)(2,1)S(1)}, u32[]{:S(2)}, u32[]{:S(2)}) collective-permute-start(bf16[256,512]{1,0:T(8,128)(2,1)} %param.13), channel_id=1, source_target_pairs={{0,0},{1,16},{2,32},{3,48},{4,64},{5,80},{6,96},{7,112},{8,128},{9... | collective-permute-start | bytes 786440 | tf_op jit(solution)/shard_map/ppermute | solution.py:112
  52.2 26.2 %all-to-all-start = ((bf16[16,512,2,8]{1,3,2,0:T(8,128)(2,1)}), bf16[16,512,2,8]{1,3,2,0:T(8,128)(2,1)S(1)}, u32[]{:S(2)}, u32[]{:S(2)}) async-start(bf16[16,512,2,8]{1,3,2,0:T(8,128)(2,1)} %broadcast_select_fusion), calls=%async_computation | async-start | bytes 524288 | tf_op jit(solution)/shard_map/all_to_all | solution.py:66
  66.6 114.7 %all-gather.5.cloned.1.call-start = ((), (), s32[]{:S(2)}) async-start(), calls=%async_computation.4 | async-start | bytes 4456448 | tf_op jit(solution)/shard_map/all_gather | solution.py:117
  79.1 12.1 %collective-permute-start.15 = (bf16[512,256]{0,1:T(8,128)(2,1)S(1)}, bf16[512,256]{0,1:T(8,128)(2,1)S(1)}, u32[]{:S(2)}, u32[]{:S(2)}) collective-permute-start(bf16[512,256]{0,1:T(8,128)(2,1)S(1)} %pad_maximum_fusion), channel_id=1, source_target_pairs={{0,128},{16,144},{32,160},{48,176},{64,192},{80,208},{96,224},{112... | collective-permute-start | bytes 786440 | tf_op jit(solution)/shard_map/ppermute | solution.py:79
  81.0 12.2 %collective-permute-start.16 = (bf16[512,256]{0,1:T(8,128)(2,1)S(1)}, bf16[512,256]{0,1:T(8,128)(2,1)S(1)}, u32[]{:S(2)}, u32[]{:S(2)}) collective-permute-start(bf16[512,256]{0,1:T(8,128)(2,1)S(1)} %pad_maximum_fusion), channel_id=1, source_target_pairs={{0,112},{16,128},{32,144},{48,160},{64,176},{80,192},{96,208},{112... | collective-permute-start | bytes 786440 | tf_op jit(solution)/shard_map/ppermute | solution.py:79
  84.6 12.7 %collective-permute-start.17 = (bf16[512,256]{0,1:T(8,128)(2,1)S(1)}, bf16[512,256]{0,1:T(8,128)(2,1)S(1)}, u32[]{:S(2)}, u32[]{:S(2)}) collective-permute-start(bf16[512,256]{0,1:T(8,128)(2,1)S(1)} %pad_maximum_fusion), channel_id=1, source_target_pairs={{0,96},{16,112},{32,128},{48,144},{64,160},{80,176},{96,192},{112,... | collective-permute-start | bytes 786440 | tf_op jit(solution)/shard_map/ppermute | solution.py:79
  87.3 11.9 %collective-permute-start.18 = (bf16[512,256]{0,1:T(8,128)(2,1)S(1)}, bf16[512,256]{0,1:T(8,128)(2,1)S(1)}, u32[]{:S(2)}, u32[]{:S(2)}) collective-permute-start(bf16[512,256]{0,1:T(8,128)(2,1)S(1)} %pad_maximum_fusion), channel_id=1, source_target_pairs={{0,80},{16,96},{32,112},{48,128},{64,144},{80,160},{96,176},{112,1... | collective-permute-start | bytes 786440 | tf_op jit(solution)/shard_map/ppermute | solution.py:79
  89.2 17.6 %collective-permute-start.19 = (bf16[512,256]{0,1:T(8,128)(2,1)S(1)}, bf16[512,256]{0,1:T(8,128)(2,1)S(1)}, u32[]{:S(2)}, u32[]{:S(2)}) collective-permute-start(bf16[512,256]{0,1:T(8,128)(2,1)S(1)} %pad_maximum_fusion), channel_id=1, source_target_pairs={{0,64},{16,80},{32,96},{48,112},{64,128},{80,144},{96,160},{112,17... | collective-permute-start | bytes 786440 | tf_op jit(solution)/shard_map/ppermute | solution.py:79
  91.2 26.9 %collective-permute-start.20 = (bf16[512,256]{0,1:T(8,128)(2,1)S(1)}, bf16[512,256]{0,1:T(8,128)(2,1)S(1)}, u32[]{:S(2)}, u32[]{:S(2)}) collective-permute-start(bf16[512,256]{0,1:T(8,128)(2,1)S(1)} %pad_maximum_fusion), channel_id=1, source_target_pairs={{0,48},{16,64},{32,80},{48,96},{64,112},{80,128},{96,144},{112,160... | collective-permute-start | bytes 786440 | tf_op jit(solution)/shard_map/ppermute | solution.py:79
  93.2 52.3 %collective-permute-start.21 = (bf16[512,256]{0,1:T(8,128)(2,1)S(1)}, bf16[512,256]{0,1:T(8,128)(2,1)S(1)}, u32[]{:S(2)}, u32[]{:S(2)}) collective-permute-start(bf16[512,256]{0,1:T(8,128)(2,1)S(1)} %pad_maximum_fusion), channel_id=1, source_target_pairs={{0,32},{16,48},{32,64},{48,80},{64,96},{80,112},{96,128},{112,144}... | collective-permute-start | bytes 786440 | tf_op jit(solution)/shard_map/ppermute | solution.py:79
  97.3 50.4 %collective-permute-start.22 = (bf16[512,256]{0,1:T(8,128)(2,1)S(1)}, bf16[512,256]{0,1:T(8,128)(2,1)S(1)}, u32[]{:S(2)}, u32[]{:S(2)}) collective-permute-start(bf16[512,256]{0,1:T(8,128)(2,1)S(1)} %pad_maximum_fusion), channel_id=1, source_target_pairs={{0,16},{16,32},{32,48},{48,64},{64,80},{80,96},{96,112},{112,128},... | collective-permute-start | bytes 786440 | tf_op jit(solution)/shard_map/ppermute | solution.py:79
  176.7 91.3 %all-to-all-start.1 = ((bf16[16,512,256]{1,2,0:T(8,128)(2,1)}), bf16[16,512,256]{1,2,0:T(8,128)(2,1)}, u32[]{:S(2)}, u32[]{:S(2)}) async-start(bf16[16,512,256]{1,2,0:T(8,128)(2,1)} %stack.71), calls=%async_computation.1 | async-start | bytes 8388608 | tf_op jit(solution)/shard_map/all_to_all | solution.py:119
  (9 other events, 57.8 us)
Sparse Core Ops, SparseCore 0:
  9.2 54.0 all-gather.2
  87.4 52.9 all-gather.4
